TPU v7x, 32 devices: a whole 2x2x4 slice. The times are simulated.
32 devices in a mesh: groups: 1, rows: 32 (over z, y, x, core).
Axes of the slice: x: 2, y: 2, z: 4, core: 2. Of those that a mesh axis runs over, the one named last changes fastest.
Arguments:
- acts: bfloat16 [4096, 2, 4096], P(('groups', 'rows')), may hold values from -6 to 6
- grads_out: bfloat16 [4096, 2, 4096], P(('groups', 'rows')), may hold values from -6 to 6
- lengths: int32 [32], P('groups'), may hold values from 1 to 512, 4096 in all
- valid: int32 [4096], P(('groups', 'rows')), may hold values 0 or 1
- proj_in: bfloat16 [4096, 128], replicated, may hold values from -0.09375 to 0.09375
- proj_out: bfloat16 [4096, 128], replicated, may hold values from -0.09375 to 0.09375
- fisher_inv: float32 [2, 4096, 4096], P(None, 'rows'), may hold values from -1 to 2, as said below
- database: float32 [4096, 2, 4096], P(('groups', 'rows')), may hold values from -250 to 250
Outputs:
- zscores: float32 [32, 4096], P(None, ('groups', 'rows'))
Inputs may be any that keep to these rules, and one draw needn't show every extreme that they name: The lengths sum to 4096; the largest is exactly 512. `fisher_inv`: each of the 2 blocks is symmetric.
All inputs are finite; a program needn't handle non-finite values. No bound on the sum of `valid` on one device may be relied on, other than what follows from the above.
Results may differ from a plain program's by a relative error of at most 0.0042.
Values sent between devices are 32-bit elements; how exact they have to be, the bound alone decides.
No kernel may reach another device: no remote copies, remote signals or barrier semaphores. Data moves between devices by JAX's collectives and lax.ppermute only.
A program may use at most 64 MiB of HBM per device.

v0:
```python
import jax
import jax.numpy as jnp
from jax import lax
from jax.sharding import PartitionSpec as P


def shards(acts, grads_out, lengths, valid, proj_in, proj_out, fisher_inv, database):
    tok_rows = acts.shape[0]
    modules = acts.shape[1]
    proj_rank = proj_in.shape[1] // modules
    queries = lengths.shape[0]
    flat_width = proj_rank * proj_rank
    first_pos = lax.axis_index("rows") * tok_rows
    positions = first_pos + jnp.arange(tok_rows, dtype=jnp.int32)
    seg_ends = jnp.cumsum(lengths)
    segment = jnp.sum((seg_ends[None, :] <= positions[:, None]).astype(jnp.int32), axis=1)
    selector = (
        (segment[:, None] == jnp.arange(queries, dtype=jnp.int32)[None, :]) & (valid[:, None] == 1)
    ).astype(jnp.bfloat16)
    module_sums = []
    for m in range(modules):
        act_proj = jnp.dot(
            acts[:, m, :],
            proj_in[:, m * proj_rank : (m + 1) * proj_rank],
            preferred_element_type=jnp.float32,
        ).astype(jnp.bfloat16)
        grad_proj = jnp.dot(
            grads_out[:, m, :],
            proj_out[:, m * proj_rank : (m + 1) * proj_rank],
            preferred_element_type=jnp.float32,
        ).astype(jnp.bfloat16)
        spread = (selector[:, :, None] * grad_proj[:, None, :]).reshape(
            tok_rows, queries * proj_rank
        )
        module_sum = lax.dot_general(
            spread, act_proj, (((0,), (0,)), ((), ())), preferred_element_type=jnp.float32
        )
        module_sums.append(module_sum.reshape(queries, flat_width))
    partial_value = jnp.stack(module_sums, axis=1)
    summed = lax.psum(partial_value, "rows")
    precond_cols = jnp.einsum("qmk,mck->qmc", summed, fisher_inv, precision=lax.Precision.HIGHEST)
    scores = jnp.einsum(
        "qmk,nmk->qn",
        lax.all_gather(precond_cols, "rows", axis=2, tiled=True),
        database,
        precision=lax.Precision.HIGHEST,
    )
    db_count = database.shape[0] * lax.axis_size("rows")
    first_moment, second_moment = lax.psum(
        (jnp.sum(scores, axis=1), jnp.sum(scores * scores, axis=1)), "rows"
    )
    avg_score = first_moment / db_count
    variance = second_moment / db_count - avg_score * avg_score
    centred = scores - avg_score[:, None]
    return centred * lax.rsqrt(variance + 1e-06)[:, None]


def solution(mesh):
    placed = (
        P(("groups", "rows"), None, None),
        P(("groups", "rows"), None, None),
        P("groups"),
        P(("groups", "rows")),
        P(),
        P(),
        P(None, "rows", None),
        P(("groups", "rows"), None, None),
    )
    return jax.shard_map(
        shards, mesh=mesh, in_specs=placed, out_specs=P(None, ("groups", "rows")), check_vma=False
    )
```

profile of v0, /device:TPU:0, one launch (start us, length us, event | category | flops | bytes accessed | tf_op | source)
XLA Modules:
  0.0 286.0 jit_solution(3558763104719825832)
XLA Ops:
  6.5 0.0 all-reduce.3.cloned.1.call-start
  6.5 0.0 copy-start.4
  6.5 6.1 %fusion.17 = (bf16[128,1,4096]{2,1,0:T(2,128)(2,1)S(1)}, bf16[128,1,4096]{2,1,0:T(2,128)(2,1)S(1)}) fusion(bf16[128,2,4096]{2,1,0:T(2,128)(2,1)} %param.9), kind=kLoop, calls=%fused_computation.33 | loop fusion | bytes 4194304 | tf_op jit(solution)/shard_map/slice | solution.py:28
  12.7 0.0 copy-done.4
  12.7 0.0 copy-start.3
  12.7 0.0 copy-start.5
  12.7 0.0 copy-start
  12.7 1.6 convolution_convert_fusion.1
  14.4 1.3 convolution_convert_fusion.3
  15.7 0.0 copy-done.3
  15.7 0.1 copy.21
  15.8 0.1 reduce-window.8
  15.8 0.1 reduce
  16.0 0.0 copy-done.5
  16.0 0.0 copy-done
  16.0 0.0 copy-start.2
  16.0 5.8 %fusion.16 = (bf16[128,1,4096]{2,1,0:T(2,128)(2,1)}, bf16[128,1,4096]{2,1,0:T(2,128)(2,1)}) fusion(bf16[128,2,4096]{2,1,0:T(2,128)(2,1)S(1)} %copy-done), kind=kLoop, calls=%fused_computation.32 | loop fusion | bytes 4194304 | tf_op jit(solution)/shard_map/slice | solution.py:23
  21.9 0.1 convert_reduce_fusion
  22.0 1.1 broadcast_multiply_fusion.1
  23.0 0.0 copy-done.2
  23.0 0.0 copy-start.1
  23.0 4.6 %fusion.2 = f32[2048,64]{1,0:T(8,128)} fusion(bf16[128,2048]{0,1:T(8,128)(2,1)} %bitcast.27, bf16[128,1,4096]{2,1,0:T(2,128)(2,1)} %get-tuple-element.9, bf16[4096,128]{1,0:T(8,128)(2,1)S(1)} %copy-done.2), kind=kOutput, calls=%fused_computation.7 | convolution fusion | flops 100671488 | bytes 3145728 | tf_op jit(solution)/shard_map/dot_general | solution.py:35
  27.6 2.4 stack_reshape.6
  30.0 0.0 copy-done.1
  30.0 4.0 %fusion.3 = f32[2048,64]{1,0:T(8,128)} fusion(bf16[128,2048]{0,1:T(8,128)(2,1)} %bitcast.26, bf16[128,1,4096]{2,1,0:T(2,128)(2,1)S(1)} %copy-done.1, bf16[4096,128]{1,0:T(8,128)(2,1)S(1)} %copy-done.2), kind=kOutput, calls=%fused_computation.8 | convolution fusion | flops 100671488 | bytes 3145728 | tf_op jit(solution)/shard_map/dot_general | solution.py:35
  34.0 1.6 stack_reshape.7
  35.6 2.1 pad_maximum_fusion
  37.7 0.0 all-reduce.3.cloned.1.call-update
  37.8 0.2 all-gather.2.cloned.1.call-start
  38.0 133.4 %all-reduce.3.cloned.1.call-done = f32[32,2,4096]{2,0,1:T(8,128)} async-done(((f32[32,2,4096]{2,0,1:T(8,128)}), f32[32,2,4096]{2,0,1:T(8,128)}) %all-reduce.3.cloned.1.call-update) | async-done | bytes 1048592 | tf_op jit(solution)/shard_map/psum | solution.py:40
  171.4 7.3 %convolution_bitcast_fusion = f32[32,2,128]{2,0,1:T(8,128)} fusion(f32[32,2,4096]{2,0,1:T(8,128)} %all-reduce.3.cloned.1.call-done, f32[2,128,4096]{2,1,0:T(8,128)} %param.14), kind=kOutput, calls=%fused_computation.2 | convolution fusion | flops 402653184 | bytes 5275648 | tf_op jit(solution)/shard_map/qmk,mck->qmc/dot_general | solution.py:41
  178.7 0.0 all-gather.2.cloned.1.call-update
  178.8 51.4 %all-gather.2.cloned.1.call-done = f32[32,2,4096]{2,0,1:T(8,128)} async-done(((f32[32,2,128]{2,0,1:T(8,128)}), f32[32,2,4096]{2,0,1:T(8,128)}) %all-gather.2.cloned.1.call-update) | async-done | bytes 1048592 | tf_op jit(solution)/shard_map/all_gather | solution.py:44
  230.2 8.2 %fusion.15 = (f32[32]{0:T(128)S(1)}, f32[32]{0:T(128)S(1)}, f32[32,128]{1,0:T(8,128)S(1)}) fusion(f32[32,2,4096]{2,0,1:T(8,128)} %all-gather.2.cloned.1.call-done, f32[128,2,4096]{2,1,0:T(2,128)} %param.15), kind=kOutput, calls=%fused_computation.31 | convolution fusion | flops 402665408 | bytes 5259520 | tf_op jit(solution)/shard_map/qmk,nmk->qn/dot_general | solution.py:42
  238.3 40.1 %all-reduce = (f32[32]{0:T(128)S(1)}, f32[32]{0:T(128)S(1)}) all-reduce(f32[32]{0:T(128)S(1)} %get-tuple-element.6, f32[32]{0:T(128)S(1)} %get-tuple-element.5), channel_id=1, replica_groups=mesh['groups'=1,'rows'=32] {'rows'}, use_global_device_ids=true, to_apply=%region_6.7 | all-reduce | flops 64 | bytes 512 | tf_op jit(solution)/shard_map/psum | solution.py:49
  278.5 0.7 subtract_multiply_fusion
  (4 shorter events, 0.0 us)
Async XLA Ops:
  6.5 164.9 %all-reduce.3.cloned.1.call-start = ((), (), s32[]{:S(2)}) async-start(), calls=%async_computation | async-start | bytes 2097152 | tf_op jit(solution)/shard_map/psum | solution.py:40
  6.5 6.1 %copy-start.4 = (bf16[4096,128]{1,0:T(8,128)(2,1)S(1)}, bf16[4096,128]{1,0:T(8,128)(2,1)}, u32[]{:S(2)}) copy-start(bf16[4096,128]{1,0:T(8,128)(2,1)} %param.13) | copy-start | bytes 3145732
  12.7 3.0 %copy-start.3 = (s32[32]{0:T(128)S(1)}, s32[32]{0:T(128)}, u32[]{:S(2)}) copy-start(s32[32]{0:T(128)} %param.10) | copy-start | bytes 388
  12.7 3.3 %copy-start.5 = (s32[128]{0:T(128)S(1)}, s32[128]{0:T(128)}, u32[]{:S(2)}) copy-start(s32[128]{0:T(128)} %param.11) | copy-start | bytes 1540
  12.7 3.3 %copy-start = (bf16[128,2,4096]{2,1,0:T(2,128)(2,1)S(1)}, bf16[128,2,4096]{2,1,0:T(2,128)(2,1)}, u32[]{:S(2)}) copy-start(bf16[128,2,4096]{2,1,0:T(2,128)(2,1)} %param.8) | copy-start | bytes 6291460
  16.0 7.0 %copy-start.2 = (bf16[4096,128]{1,0:T(8,128)(2,1)S(1)}, bf16[4096,128]{1,0:T(8,128)(2,1)}, u32[]{:S(2)}) copy-start(bf16[4096,128]{1,0:T(8,128)(2,1)} %param.12) | copy-start | bytes 3145732
  23.0 7.0 %copy-start.1 = (bf16[128,1,4096]{2,1,0:T(2,128)(2,1)S(1)}, bf16[128,1,4096]{2,1,0:T(2,128)(2,1)}, u32[]{:S(2)}) copy-start(bf16[128,1,4096]{2,1,0:T(2,128)(2,1)} %get-tuple-element.10) | copy-start | bytes 3145732
  37.8 192.4 %all-gather.2.cloned.1.call-start = ((), (), s32[]{:S(2)}) async-start(), calls=%async_computation.1 | async-start | bytes 1081344 | tf_op jit(solution)/shard_map/all_gather | solution.py:44
Sparse Core Ops, SparseCore 0:
  37.9 133.4 all-reduce.2
  178.9 51.2 all-gather.1
where the time goes:
time: 286 us
  waiting for transfers between devices  185 us (65%)
  blocking collectives  40.1 us (14%)
  matrix products  27.1 us (9%)
  local copies, waits for them, and re-layouts  16 us (6%)
  between operations  13.5 us (5%)
  other arithmetic  4.19 us (1%)
    psum x1, waiting for transfers between devices, shards(): summed = lax.psum(partial_value, 'rows')  133 us
    all_gather x1, waiting for transfers between devices, shards(): lax.all_gather(precond_cols, 'rows', axis=2, tiled=True)  51.4 us
    psum x1, blocking collectives, shards(): lax.psum((jnp.sum(scores, axis=1), jnp.sum(scores * scores, axis=1)), 'ro...  40.1 us
    dot_general x2, matrix products, shards(): lax.dot_general(spread, act_proj, (((0,), (0,)), ((), ())), preferred_ele...  8.6 us
    dot_general x1, matrix products, shards(): jnp.einsum('qmk,nmk->qn', lax.all_gather(precond_cols, 'rows', axis=2, ti...  8.16 us
    dot_general x1, matrix products, shards(): jnp.einsum('qmk,mck->qmc', summed, fisher_inv, precision=lax.Precision.HI...  7.35 us
    slice x1, local copies, waits for them, and re-layouts, shards(): grads_out[:, m, :]  6.11 us
    slice x1, local copies, waits for them, and re-layouts, shards(): acts[:, m, :]  5.84 us
  transfers between devices with their start and end apart: 2, of which 2 were waited for; matrix products, arithmetic and copies ran while one was open for 0% of the time, Pallas kernels for 0%

commit v1 on v0

--- a/solution.py
+++ b/solution.py
@@ -2,6 +2,7 @@
 import jax.numpy as jnp
 from jax import lax
 from jax.sharding import PartitionSpec as P
+from jax.lax import all_gather
 
 
 def shards(acts, grads_out, lengths, valid, proj_in, proj_out, fisher_inv, database):
@@ -37,7 +38,11 @@
         )
         module_sums.append(module_sum.reshape(queries, flat_width))
     partial_value = jnp.stack(module_sums, axis=1)
-    summed = lax.psum(partial_value, "rows")
+
+    def work_the_outputs(unit):
+        return all_gather(unit, axis_name="rows").sum(axis=0)
+
+    summed = work_the_outputs(partial_value)
     precond_cols = jnp.einsum("qmk,mck->qmc", summed, fisher_inv, precision=lax.Precision.HIGHEST)
     scores = jnp.einsum(
         "qmk,nmk->qn",

time: 286 us -> 362 us (1.27)
  waiting for transfers between devices: 185 us -> 248 us
  other arithmetic: 4.19 us -> 16.4 us
    all_gather x0 -> x1, waiting for transfers between devices: none -> 197 us  [work_the_outputs(): return all_gather(unit, axis_name='rows').sum(axis=0)]
    psum x1 -> x0, waiting for transfers between devices: 133 us -> none  [shards(): summed = lax.psum(partial_value, 'rows')]
    reduce_sum x0 -> x1, other arithmetic: none -> 11.7 us  [work_the_outputs(): return all_gather(unit, axis_name='rows').sum(axis=0)]
where the time goes in v1:
time: 362 us; the launch traced here: 361 us
  waiting for transfers between devices  248 us (69%)
  blocking collectives  40.1 us (11%)
  matrix products  26.1 us (7%)
  local copies, waits for them, and re-layouts  17.2 us (5%)
  other arithmetic  16.4 us (5%)
  between operations  13.5 us (4%)
    all_gather x1, waiting for transfers between devices, work_the_outputs(): return all_gather(unit, axis_name='rows').sum(axis=0)  197 us
    all_gather x1, waiting for transfers between devices, shards(): lax.all_gather(precond_cols, 'rows', axis=2, tiled=True)  50.6 us
    psum x1, blocking collectives, shards(): lax.psum((jnp.sum(scores, axis=1), jnp.sum(scores * scores, axis=1)), 'ro...  40.1 us
    reduce_sum x1, other arithmetic, work_the_outputs(): return all_gather(unit, axis_name='rows').sum(axis=0)  11.7 us
    dot_general x2, matrix products, shards(): lax.dot_general(spread, act_proj, (((0,), (0,)), ((), ())), preferred_ele...  8.48 us
    dot_general x1, matrix products, shards(): jnp.einsum('qmk,nmk->qn', lax.all_gather(precond_cols, 'rows', axis=2, ti...  8.16 us
    slice x1, local copies, waits for them, and re-layouts, shards(): acts[:, m, :]  7.65 us
  transfers between devices with their start and end apart: 2, of which 2 were waited for; matrix products, arithmetic and copies ran while one was open for 0% of the time, Pallas kernels for 0%

profile of v1, /device:TPU:0, one launch (start us, length us, event | category | flops | bytes accessed | tf_op | source)
XLA Modules:
  0.0 361.1 jit_solution(4628926813735376383)
XLA Ops:
  6.5 0.0 all-gather.6.cloned.1.call-start
  6.5 0.7 broadcast_compare_fusion
  7.2 0.7 copy.29
  7.9 0.1 reduce-window.8
  8.0 0.1 reduce
  8.1 0.0 copy-start
  8.1 7.6 %fusion.16 = (bf16[128,1,4096]{2,1,0:T(2,128)(2,1)}, bf16[128,1,4096]{2,1,0:T(2,128)(2,1)S(1)}) fusion(bf16[128,2,4096]{2,1,0:T(2,128)(2,1)} %param.8), kind=kLoop, calls=%fused_computation.32 | loop fusion | bytes 4194304 | tf_op jit(solution)/shard_map/slice | solution.py:24
  15.8 0.0 copy-done
  15.8 0.0 copy-start.2
  15.8 4.8 %fusion.17 = (bf16[128,1,4096]{2,1,0:T(2,128)(2,1)S(1)}, bf16[128,1,4096]{2,1,0:T(2,128)(2,1)S(1)}) fusion(bf16[128,2,4096]{2,1,0:T(2,128)(2,1)S(1)} %copy-done), kind=kLoop, calls=%fused_computation.33 | loop fusion | bytes 4194304 | tf_op jit(solution)/shard_map/slice | solution.py:29
  20.6 0.0 copy-done.2
  20.6 1.3 convolution_convert_fusion.3
  21.9 0.0 copy-start.1
  22.0 1.6 convolution_convert_fusion.1
  23.6 0.1 convert_reduce_fusion
  23.7 1.0 broadcast_multiply_fusion.1
  24.7 0.0 copy-done.1
  24.7 4.5 %fusion.2 = f32[2048,64]{1,0:T(8,128)} fusion(bf16[128,2048]{0,1:T(8,128)(2,1)} %bitcast.29, bf16[128,1,4096]{2,1,0:T(2,128)(2,1)} %get-tuple-element.9, bf16[4096,128]{1,0:T(8,128)(2,1)S(1)} %copy-done.1), kind=kOutput, calls=%fused_computation.7 | convolution fusion | flops 100671488 | bytes 3145728 | tf_op jit(solution)/shard_map/dot_general | solution.py:36
  29.2 2.4 stack_reshape.6
  31.6 4.0 %fusion.3 = f32[2048,64]{1,0:T(8,128)} fusion(bf16[128,2048]{0,1:T(8,128)(2,1)} %bitcast.28, bf16[128,1,4096]{2,1,0:T(2,128)(2,1)S(1)} %get-tuple-element.10, bf16[4096,128]{1,0:T(8,128)(2,1)S(1)} %copy-done.1), kind=kOutput, calls=%fused_computation.8 | convolution fusion | flops 100671488 | bytes 3145728 | tf_op jit(solution)/shard_map/dot_general | solution.py:36
  35.6 1.6 stack_reshape.7
  37.2 2.1 pad_maximum_fusion
  39.3 0.0 all-gather.6.cloned.1.call-update
  39.3 0.2 all-gather.4.cloned.1.call-start
  39.6 196.9 %all-gather.6.cloned.1.call-done = f32[1024,2,4096]{2,0,1:T(8,128)} async-done(((f32[32,2,4096]{2,0,1:T(8,128)}), f32[1024,2,4096]{2,0,1:T(8,128)}) %all-gather.6.cloned.1.call-update) | async-done | bytes 33554448 | tf_op jit(solution)/shard_map/all_gather | solution.py:43
  236.4 11.7 %reduce_sum.37 = f32[32,2,4096]{2,0,1:T(8,128)S(1)} reduce(f32[32,32,2,4096]{3,1,0,2:T(8,128)} %bitcast.27, f32[]{:T(128)} %constant.18.clone.1), dimensions={0}, to_apply=%region_2.3 | reduce | flops 8126464 | bytes 34603012 | tf_op jit(solution)/shard_map/reduce_sum | solution.py:43
  248.1 6.5 %convolution_bitcast_fusion = f32[32,2,128]{2,0,1:T(8,128)} fusion(f32[32,2,4096]{2,0,1:T(8,128)S(1)} %reduce_sum.37, f32[2,128,4096]{2,1,0:T(8,128)} %param.14), kind=kOutput, calls=%fused_computation.2 | convolution fusion | flops 402653184 | bytes 5275648 | tf_op jit(solution)/shard_map/qmk,mck->qmc/dot_general | solution.py:46
  254.6 0.0 all-gather.4.cloned.1.call-update
  254.6 50.6 %all-gather.4.cloned.1.call-done = f32[32,2,4096]{2,0,1:T(8,128)} async-done(((f32[32,2,128]{2,0,1:T(8,128)}), f32[32,2,4096]{2,0,1:T(8,128)}) %all-gather.4.cloned.1.call-update) | async-done | bytes 1048592 | tf_op jit(solution)/shard_map/all_gather | solution.py:49
  305.2 8.2 %fusion.15 = (f32[32]{0:T(128)S(1)}, f32[32]{0:T(128)S(1)}, f32[32,128]{1,0:T(8,128)S(1)}) fusion(f32[32,2,4096]{2,0,1:T(8,128)} %all-gather.4.cloned.1.call-done, f32[128,2,4096]{2,1,0:T(2,128)} %param.15), kind=kOutput, calls=%fused_computation.31 | convolution fusion | flops 402665408 | bytes 5259520 | tf_op jit(solution)/shard_map/qmk,nmk->qn/dot_general | solution.py:47
  313.4 40.1 %all-reduce = (f32[32]{0:T(128)S(1)}, f32[32]{0:T(128)S(1)}) all-reduce(f32[32]{0:T(128)S(1)} %get-tuple-element.6, f32[32]{0:T(128)S(1)} %get-tuple-element.5), channel_id=1, replica_groups=mesh['groups'=1,'rows'=32] {'rows'}, use_global_device_ids=true, to_apply=%region_6.7 | all-reduce | flops 64 | bytes 512 | tf_op jit(solution)/shard_map/psum | solution.py:54
  353.5 0.7 subtract_multiply_fusion
  (3 shorter events, 0.0 us)
Async XLA Ops:
  6.5 229.9 %all-gather.6.cloned.1.call-start = ((), (), s32[]{:S(2)}) async-start(), calls=%async_computation.1 | async-start | bytes 34603008 | tf_op jit(solution)/shard_map/all_gather | solution.py:43
  8.1 7.7 %copy-start = (bf16[128,2,4096]{2,1,0:T(2,128)(2,1)S(1)}, bf16[128,2,4096]{2,1,0:T(2,128)(2,1)}, u32[]{:S(2)}) copy-start(bf16[128,2,4096]{2,1,0:T(2,128)(2,1)} %param.9) | copy-start | bytes 6291460
  15.8 4.8 %copy-start.2 = (bf16[4096,128]{1,0:T(8,128)(2,1)S(1)}, bf16[4096,128]{1,0:T(8,128)(2,1)}, u32[]{:S(2)}) copy-start(bf16[4096,128]{1,0:T(8,128)(2,1)} %param.13) | copy-start | bytes 3145732
  21.9 2.8 copy-start.1
  39.3 265.9 %all-gather.4.cloned.1.call-start = ((), (), s32[]{:S(2)}) async-start(), calls=%async_computation | async-start | bytes 1081344 | tf_op jit(solution)/shard_map/all_gather | solution.py:49
Sparse Core Ops, SparseCore 0:
  39.4 196.9 all-gather.5
  254.7 50.4 all-gather.3
